TPU v7x, 512 devices: a whole 4x4x16 slice. The times are simulated.
512 devices in a mesh: section: 8 (over x, y_hi), vocab: 64 (over z, y_lo, core).
Axes of the slice: x: 4, y: 4 (y_hi: 2, y_lo: 2; y = y_hi * 2 + y_lo), z: 16, core: 2. Of those that a mesh axis runs over, the one named last changes fastest.
Arguments:
- hidden: bfloat16 [512, 8192], P('vocab', 'section'), may hold values from -6 to 6
- head_weight: bfloat16 [98304, 8192], P('vocab', 'section'), may hold values from -3 to 3
- lengths: int32 [8], replicated, may hold values from 16 to 64
- pairing: int32 [4], replicated, may hold values from 0 to 3, each once
Outputs:
- hidden_grad: float32 [512, 8192], P('vocab', 'section')
- loss: float32 [], replicated
Inputs may be any that keep to these rules, and one draw needn't show every extreme that they name: Every sequence has at least one live token; positions from lengths on are padding. `pairing`: a permutation: each document matches exactly one query.
All inputs are finite; a program needn't handle non-finite values.
Results may differ from a plain program's by a relative error of at most 0.0018.
Values may be sent and summed in bfloat16 or wider, within the bound.
No kernel may reach another device: no remote copies, remote signals or barrier semaphores. Data moves between devices by JAX's collectives and lax.ppermute only.
A program may use at most 64 MiB of HBM per device.

v0:
```python
import jax
import jax.numpy as jnp
from jax import lax
from jax.sharding import PartitionSpec as P

NSEQ = 8
pool_temp = 0.5
score_temp = 0.02
grad_scale = 16.0
eps_norm = 1e-06


def local(hidden, head_weight, lengths, pairing):
    half = NSEQ // 2
    partial_logits = lax.dot_general(
        lax.all_gather(hidden, "vocab", axis=0, tiled=True),
        head_weight,
        (((1,), (1,)), ((), ())),
        preferred_element_type=jnp.float32,
    )
    total_rows = partial_logits.shape[0]
    seq_len = total_rows // NSEQ
    logits = lax.psum(partial_logits, "section")
    columns = logits.shape[1]
    soft = jax.nn.softplus(logits)
    act = jnp.log1p(soft)
    positions = jnp.arange(seq_len, dtype=jnp.int32)
    live = (positions[None, :] < lengths[:, None]).astype(jnp.float32)
    expo = jnp.exp(act / pool_temp).reshape(NSEQ, seq_len, columns) * live[:, :, None]
    totals = jnp.sum(expo, axis=1)
    pooled = pool_temp * jnp.log(totals)
    queries = pooled[:half]
    documents = pooled[half:]
    dots_part = lax.dot_general(
        queries, documents, (((1,), (1,)), ((), ())), precision=lax.Precision.HIGHEST
    )
    norms_part = jnp.sum(pooled * pooled, axis=1)
    dots, norms = lax.psum((dots_part, norms_part), "vocab")
    inv = lax.rsqrt(norms + eps_norm)
    inv_q = inv[:half]
    inv_d = inv[half:]
    scores = dots * inv_q[:, None] * inv_d[None, :] / score_temp
    weights = jnp.exp(scores)
    row_sum = jnp.sum(weights, axis=1)
    probs = weights / row_sum[:, None]
    target = (jnp.arange(half, dtype=jnp.int32)[None, :] == pairing[:, None]).astype(jnp.float32)
    loss = jnp.sum(jnp.log(row_sum) - jnp.sum(scores * target, axis=1))
    dscore = grad_scale * (probs - target)
    gdots = dscore * inv_q[:, None] * inv_d[None, :] / score_temp
    dinv_q = jnp.sum(dscore * dots * inv_d[None, :], axis=1) / score_temp
    dinv_d = jnp.sum(dscore * dots * inv_q[:, None], axis=0) / score_temp
    dinv = jnp.concatenate([dinv_q, dinv_d])
    dnorm = -0.5 * dinv * inv * inv * inv
    dpool_q = (
        jnp.dot(gdots, documents, precision=lax.Precision.HIGHEST)
        + 2.0 * dnorm[:half, None] * queries
    )
    dpool_d = (
        jnp.dot(gdots.T, queries, precision=lax.Precision.HIGHEST)
        + 2.0 * dnorm[half:, None] * documents
    )
    dpooled = jnp.concatenate([dpool_q, dpool_d], axis=0)
    dact = (dpooled[:, None, :] * expo / totals[:, None, :]).reshape(total_rows, columns)
    dlogit = (dact * jax.nn.sigmoid(logits) / (1.0 + soft)).astype(jnp.bfloat16)
    hidden_grad = lax.psum_scatter(
        jnp.dot(dlogit, head_weight, preferred_element_type=jnp.float32),
        "vocab",
        scatter_dimension=0,
        tiled=True,
    )
    return (hidden_grad, loss)


def solution(mesh):
    in_specs = (P("vocab", "section"), P("vocab", "section"), P(), P())
    out_specs = (P("vocab", "section"), P())
    return jax.shard_map(local, mesh=mesh, in_specs=in_specs, out_specs=out_specs, check_vma=False)
```

profile of v0, /device:TPU:2, one launch (start us, length us, event | category | flops | bytes accessed | tf_op | source)
XLA Modules:
  0.0 654.5 jit_solution(2297248620862196060)
XLA Ops:
  7.2 0.7 all-gather.2.cloned.1.call-update
  7.9 0.0 all-reduce.3.cloned.1.call-start
  8.0 127.2 %all-gather.2.cloned.1.call-done = bf16[512,1024]{1,0:T(8,128)(2,1)} async-done(((bf16[8,1024]{1,0:T(8,128)(2,1)}), bf16[512,1024]{1,0:T(8,128)(2,1)}) %all-gather.2.cloned.1.call-update) | async-done | bytes 1048592 | tf_op jit(solution)/shard_map/all_gather | solution.py:16
  135.2 4.7 fusion.17
  140.0 0.0 reduce-scatter.2.cloned.1.call-start
  140.0 0.6 copy-done.1
  140.6 0.1 fusion.8
  140.7 0.1 reshape.50
  140.7 157.0 %all-reduce.3.cloned.1.call-done = f32[512,1536]{1,0:T(8,128)} async-done(((f32[512,1536]{1,0:T(8,128)}), f32[512,1536]{1,0:T(8,128)}) %all-reduce.3.cloned.1.call-update) | async-done | bytes 3145744 | tf_op jit(solution)/shard_map/psum | solution.py:23
  297.7 5.1 multiply_reduce_fusion
  302.8 0.1 multiply_reduce_fusion.1
  302.9 0.2 fusion.4
  303.1 108.1 %all-reduce = (f32[8]{0:T(128)S(1)}, f32[4,4]{1,0:T(4,128)S(1)}) all-reduce(f32[8]{0:T(128)S(1)} %get-tuple-element.8, f32[4,4]{1,0:T(4,128)S(1)} %fusion.4), channel_id=1, replica_groups=mesh['section'=8,'vocab'=64] {'vocab'}, use_global_device_ids=true, to_apply=%region_4.5 | all-reduce | flops 24 | bytes 192 | tf_op jit(solution)/shard_map/psum | solution.py:38
  411.2 0.1 broadcast_multiply_fusion.2
  411.3 0.2 exponential_reduce_fusion
  411.5 0.2 multiply_reduce_fusion.3
  411.7 0.1 multiply_multiply_fusion.5
  411.7 0.1 slice_multiply_fusion.1
  411.8 0.2 convolution_add_fusion.1
  412.1 0.3 convolution_add_fusion
  412.4 5.5 fusion.2
  418.0 3.2 fusion.18
  421.2 0.6 subtract_reduce_fusion
  421.8 226.2 %reduce-scatter.2.cloned.1.call-done = f32[8,1024]{1,0:T(8,128)} async-done(((f32[512,1024]{1,0:T(8,128)}), f32[8,1024]{1,0:T(8,128)}) %reduce-scatter.2.cloned.1.call-update) | async-done | bytes 32784 | tf_op jit(solution)/shard_map/reduce_scatter | solution.py:65
  (11 shorter events, 0.1 us)
Async XLA Ops:
  7.2 128.0 %copy-start = (bf16[1536,1024]{1,0:T(8,128)(2,1)S(1)}, bf16[1536,1024]{1,0:T(8,128)(2,1)}, u32[]{:S(2)}) copy-start(bf16[1536,1024]{1,0:T(8,128)(2,1)} %param.5) | copy-start | bytes 9437188
  7.2 128.0 %all-gather.2.cloned.1.call-start = ((), (), s32[]{:S(2)}) async-start(), calls=%async_computation.1 | async-start | bytes 1064960 | tf_op jit(solution)/shard_map/all_gather | solution.py:16
  7.9 289.8 %all-reduce.3.cloned.1.call-start = ((), (), s32[]{:S(2)}) async-start(), calls=%async_computation.2 | async-start | bytes 6291456 | tf_op jit(solution)/shard_map/psum | solution.py:23
  139.9 0.7 copy-start.1
  140.0 271.5 %copy-start.2 = (s32[4]{0:T(128)S(1)}, s32[4]{0:T(128)}, u32[]{:S(2)}) copy-start(s32[4]{0:T(128)} %param.7) | copy-start | bytes 52
  140.0 508.0 %reduce-scatter.2.cloned.1.call-start = ((), (), s32[]{:S(2)}) async-start(), calls=%async_computation.3 | async-start | bytes 2129920 | tf_op jit(solution)/shard_map/reduce_scatter | solution.py:65
Sparse Core Ops, SparseCore 0:
  10.2 124.9 all-gather.1
  140.1 157.6 all-reduce.2
  421.3 226.6 reduce-scatter.1
where the time goes:
time: 655 us
  waiting for transfers between devices  511 us (78%)
  blocking collectives  108 us (16%)
  between operations  13.8 us (2%)
  other arithmetic  12 us (2%)
  matrix products  8.66 us (1%)
    reduce_scatter x1, waiting for transfers between devices, local(): lax.psum_scatter(jnp.dot(dlogit, head_weight, preferred_element_type=jnp....  226 us
    psum x1, waiting for transfers between devices, local(): logits = lax.psum(partial_logits, 'section')  157 us
    all_gather x1, waiting for transfers between devices, local(): lax.all_gather(hidden, 'vocab', axis=0, tiled=True)  127 us
    psum x1, blocking collectives, local(): dots, norms = lax.psum((dots_part, norms_part), 'vocab')  108 us
  transfers between devices with their start and end apart: 3, of which 3 were waited for; matrix products, arithmetic and copies ran while one was open for 0% of the time, Pallas kernels for 0%

commit v1 on v0

--- a/solution.py
+++ b/solution.py
@@ -20,7 +20,7 @@
     )
     total_rows = partial_logits.shape[0]
     seq_len = total_rows // NSEQ
-    logits = lax.psum(partial_logits, "section")
+    logits = jnp.sum(lax.all_gather(partial_logits, "section"), axis=0)
     columns = logits.shape[1]
     soft = jax.nn.softplus(logits)
     act = jnp.log1p(soft)

time: 655 us -> 781 us (1.19)
  waiting for transfers between devices: 511 us -> 625 us
  other arithmetic: 12 us -> 24 us
    all_gather x0 -> x1, waiting for transfers between devices: none -> 273 us  [local(): logits = jnp.sum(lax.all_gather(partial_logits, 'section'), axis=0)]
    psum x1 -> x0, waiting for transfers between devices: 157 us -> none  [local(): logits = lax.psum(partial_logits, 'section')]
    reduce_sum x0 -> x1, other arithmetic: none -> 11.9 us  [local(): logits = jnp.sum(lax.all_gather(partial_logits, 'section'), axis=0)]
where the time goes in v1:
time: 781 us; the launch traced here: 780 us
  waiting for transfers between devices  625 us (80%)
  blocking collectives  108 us (14%)
  other arithmetic  24 us (3%)
  between operations  13.8 us (2%)
  matrix products  8.75 us (1%)
    all_gather x1, waiting for transfers between devices, local(): logits = jnp.sum(lax.all_gather(partial_logits, 'section'), axis=0)  273 us
    reduce_scatter x1, waiting for transfers between devices, local(): lax.psum_scatter(jnp.dot(dlogit, head_weight, preferred_element_type=jnp....  224 us
    all_gather x1, waiting for transfers between devices, local(): lax.all_gather(hidden, 'vocab', axis=0, tiled=True)  127 us
    psum x1, blocking collectives, local(): dots, norms = lax.psum((dots_part, norms_part), 'vocab')  108 us
  transfers between devices with their start and end apart: 3, of which 3 were waited for; matrix products, arithmetic and copies ran while one was open for 0% of the time, Pallas kernels for 0%

profile of v1, /device:TPU:2, one launch (start us, length us, event | category | flops | bytes accessed | tf_op | source)
XLA Modules:
  0.0 780.5 jit_solution(6300930750134485920)
XLA Ops:
  7.2 0.7 all-gather.4.cloned.1.call-update
  8.0 127.2 %all-gather.4.cloned.1.call-done = bf16[512,1024]{1,0:T(8,128)(2,1)} async-done(((bf16[8,1024]{1,0:T(8,128)(2,1)}), bf16[512,1024]{1,0:T(8,128)(2,1)}) %all-gather.4.cloned.1.call-update) | async-done | bytes 1048592 | tf_op jit(solution)/shard_map/all_gather | solution.py:16
  135.2 4.8 fusion.22
  140.0 0.0 reduce-scatter.2.cloned.1.call-start
  140.1 0.6 copy-done.1
  140.7 0.1 fusion.13
  140.7 0.1 reshape.48
  140.8 273.0 %all-gather.6.cloned.1.call-done = f32[4096,1536]{1,0:T(8,128)} async-done(((f32[512,1536]{1,0:T(8,128)}), f32[4096,1536]{1,0:T(8,128)}) %all-gather.6.cloned.1.call-update) | async-done | bytes 25165840 | tf_op jit(solution)/shard_map/all_gather | solution.py:23
  413.8 11.9 %reduce_sum.74 = f32[512,1536]{1,0:T(8,128)} reduce(f32[8,512,1536]{2,1,0:T(8,128)} %bitcast.24, f32[]{:T(128)} %constant.8.clone.1), dimensions={0}, to_apply=%region_0.0 | reduce | flops 5505024 | bytes 28311556 | tf_op jit(solution)/shard_map/reduce_sum | solution.py:23
  425.8 5.1 fusion.4
  430.8 0.1 multiply_reduce_fusion
  431.0 0.2 fusion.9
  431.1 107.8 %all-reduce = (f32[8]{0:T(128)S(1)}, f32[4,4]{1,0:T(4,128)S(1)}) all-reduce(f32[8]{0:T(128)S(1)} %get-tuple-element.8, f32[4,4]{1,0:T(4,128)S(1)} %fusion.9), channel_id=1, replica_groups=mesh['section'=8,'vocab'=64] {'vocab'}, use_global_device_ids=true, to_apply=%region_4.5 | all-reduce | flops 24 | bytes 192 | tf_op jit(solution)/shard_map/psum | solution.py:38
  538.9 0.1 broadcast_multiply_fusion.2
  539.0 0.2 exponential_reduce_fusion
  539.2 0.2 multiply_reduce_fusion.2
  539.4 0.1 multiply_multiply_fusion.5
  539.5 0.1 slice_multiply_fusion.1
  539.6 0.3 convolution_add_fusion.1
  539.8 0.3 convolution_add_fusion
  540.2 5.5 fusion.7
  545.7 3.2 fusion.23
  548.9 0.6 subtract_reduce_fusion
  549.6 224.4 %reduce-scatter.2.cloned.1.call-done = f32[8,1024]{1,0:T(8,128)} async-done(((f32[512,1024]{1,0:T(8,128)}), f32[8,1024]{1,0:T(8,128)}) %reduce-scatter.2.cloned.1.call-update) | async-done | bytes 32784 | tf_op jit(solution)/shard_map/reduce_scatter | solution.py:65
  (12 shorter events, 0.2 us)
Async XLA Ops:
  7.2 128.0 %copy-start = (bf16[1536,1024]{1,0:T(8,128)(2,1)S(1)}, bf16[1536,1024]{1,0:T(8,128)(2,1)}, u32[]{:S(2)}) copy-start(bf16[1536,1024]{1,0:T(8,128)(2,1)} %param.5) | copy-start | bytes 9437188
  7.2 128.0 %all-gather.4.cloned.1.call-start = ((), (), s32[]{:S(2)}) async-start(), calls=%async_computation.1 | async-start | bytes 1064960 | tf_op jit(solution)/shard_map/all_gather | solution.py:16
  7.9 405.9 %all-gather.6.cloned.1.call-start = ((), (), s32[]{:S(2)}) async-start(), calls=%async_computation.3 | async-start | bytes 28311552 | tf_op jit(solution)/shard_map/all_gather | solution.py:23
  140.0 0.7 copy-start.1
  140.0 633.9 %reduce-scatter.2.cloned.1.call-start = ((), (), s32[]{:S(2)}) async-start(), calls=%async_computation.2 | async-start | bytes 2129920 | tf_op jit(solution)/shard_map/reduce_scatter | solution.py:65
  425.8 113.4 %copy-start.2 = (s32[4]{0:T(128)S(1)}, s32[4]{0:T(128)}, u32[]{:S(2)}) copy-start(s32[4]{0:T(128)} %param.7) | copy-start | bytes 52
Sparse Core Ops, SparseCore 0:
  10.2 124.9 all-gather.3
  140.2 273.6 all-gather.5
  549.1 224.8 reduce-scatter.1

commit v2 on v0

--- a/solution.py
+++ b/solution.py
@@ -13,7 +13,9 @@
 def local(hidden, head_weight, lengths, pairing):
     half = NSEQ // 2
     partial_logits = lax.dot_general(
-        lax.all_gather(hidden, "vocab", axis=0, tiled=True),
+        jnp.concatenate(
+            lax.all_to_all(jnp.stack([hidden] * lax.axis_size("vocab")), "vocab", 0, 0), axis=0
+        ),
         head_weight,
         (((1,), (1,)), ((), ())),
         preferred_element_type=jnp.float32,

time: 655 us -> 596 us (0.910)
  waiting for transfers between devices: 511 us -> 379 us
  blocking collectives: 108 us -> 181 us
    all_gather x1 -> x0, waiting for transfers between devices: 127 us -> none  [local(): lax.all_gather(hidden, 'vocab', axis=0, tiled=True)]
    all_to_all x0 -> x1, blocking collectives: none -> 73.1 us  [local(): lax.all_to_all(jnp.stack([hidden] * lax.axis_size('vocab')), 'vocab', 0, 0)]
  transfers between devices with their start and end apart: 3 -> 2, of which waited for: 3 -> 2; matrix products, arithmetic and copies ran while one was open for 0% -> 0% of each run, Pallas kernels for 0% -> 0%
where the time goes in v2:
time: 596 us
  waiting for transfers between devices  379 us (64%)
  blocking collectives  181 us (30%)
  between operations  14.1 us (2%)
  other arithmetic  12 us (2%)
  matrix products  7.5 us (1%)
    reduce_scatter x1, waiting for transfers between devices, local(): lax.psum_scatter(jnp.dot(dlogit, head_weight, preferred_element_type=jnp....  226 us
    psum x1, waiting for transfers between devices, local(): logits = lax.psum(partial_logits, 'section')  153 us
    psum x1, blocking collectives, local(): dots, norms = lax.psum((dots_part, norms_part), 'vocab')  108 us
    all_to_all x1, blocking collectives, local(): lax.all_to_all(jnp.stack([hidden] * lax.axis_size('vocab')), 'vocab', 0, 0)  73.1 us
  transfers between devices with their start and end apart: 2, of which 2 were waited for; matrix products, arithmetic and copies ran while one was open for 0% of the time, Pallas kernels for 0%

profile of v2, /device:TPU:2, one launch (start us, length us, event | category | flops | bytes accessed | tf_op | source)
XLA Modules:
  0.0 595.6 jit_solution(6950216735271630731)
XLA Ops:
  7.2 0.0 all-reduce.3.cloned.1.call-start
  7.2 1.0 stack.2
  8.2 73.1 %all_to_all.5 = bf16[64,8,1024]{2,1,0:T(8,128)(2,1)S(1)} all-to-all(bf16[64,8,1024]{2,1,0:T(8,128)(2,1)S(1)} %stack.2), channel_id=1, replica_groups=mesh['section'=8,'vocab'=64] {'vocab'}, dimensions={0} | all-to-all | bytes 2097152 | tf_op jit(solution)/shard_map/all_to_all | solution.py:17
  81.3 3.6 fusion.3
  84.9 0.0 reduce-scatter.2.cloned.1.call-start
  84.9 0.6 copy-done.1
  85.5 0.1 fusion.10
  85.6 0.1 reshape.56
  85.6 152.9 %all-reduce.3.cloned.1.call-done = f32[512,1536]{1,0:T(8,128)} async-done(((f32[512,1536]{1,0:T(8,128)}), f32[512,1536]{1,0:T(8,128)}) %all-reduce.3.cloned.1.call-update) | async-done | bytes 3145744 | tf_op jit(solution)/shard_map/psum | solution.py:25
  238.5 5.1 multiply_reduce_fusion
  243.6 0.1 multiply_reduce_fusion.1
  243.7 0.2 fusion.6
  243.9 108.1 %all-reduce = (f32[8]{0:T(128)S(1)}, f32[4,4]{1,0:T(4,128)S(1)}) all-reduce(f32[8]{0:T(128)S(1)} %get-tuple-element.8, f32[4,4]{1,0:T(4,128)S(1)} %fusion.6), channel_id=1, replica_groups=mesh['section'=8,'vocab'=64] {'vocab'}, use_global_device_ids=true, to_apply=%region_4.5 | all-reduce | flops 24 | bytes 192 | tf_op jit(solution)/shard_map/psum | solution.py:40
  351.9 0.1 broadcast_multiply_fusion.2
  352.0 0.2 exponential_reduce_fusion
  352.2 0.2 multiply_reduce_fusion.3
  352.4 0.1 multiply_multiply_fusion.5
  352.5 0.1 slice_multiply_fusion.1
  352.6 0.2 convolution_add_fusion.1
  352.8 0.3 convolution_add_fusion
  353.2 5.5 fusion.2
  358.7 3.2 fusion.19
  362.0 0.6 subtract_reduce_fusion
  362.6 226.2 %reduce-scatter.2.cloned.1.call-done = f32[8,1024]{1,0:T(8,128)} async-done(((f32[512,1024]{1,0:T(8,128)}), f32[8,1024]{1,0:T(8,128)}) %reduce-scatter.2.cloned.1.call-update) | async-done | bytes 32784 | tf_op jit(solution)/shard_map/reduce_scatter | solution.py:67
  (10 shorter events, 0.1 us)
Async XLA Ops:
  7.2 74.1 %copy-start = (bf16[1536,1024]{1,0:T(8,128)(2,1)S(1)}, bf16[1536,1024]{1,0:T(8,128)(2,1)}, u32[]{:S(2)}) copy-start(bf16[1536,1024]{1,0:T(8,128)(2,1)} %param.5) | copy-start | bytes 9437188
  7.2 231.3 %all-reduce.3.cloned.1.call-start = ((), (), s32[]{:S(2)}) async-start(), calls=%async_computation.2 | async-start | bytes 6291456 | tf_op jit(solution)/shard_map/psum | solution.py:25
  84.8 0.7 copy-start.1
  84.9 267.4 %copy-start.2 = (s32[4]{0:T(128)S(1)}, s32[4]{0:T(128)}, u32[]{:S(2)}) copy-start(s32[4]{0:T(128)} %param.7) | copy-start | bytes 52
  84.9 503.9 %reduce-scatter.2.cloned.1.call-start = ((), (), s32[]{:S(2)}) async-start(), calls=%async_computation.3 | async-start | bytes 2129920 | tf_op jit(solution)/shard_map/reduce_scatter | solution.py:67
Sparse Core Ops, SparseCore 0:
  85.0 153.4 all-reduce.2
  362.1 226.6 reduce-scatter.1
